TPU v7x, 128 devices: a whole 4x4x4 slice. The times are simulated.
128 devices in a mesh: grp: 4 (over x), tok: 32 (over z, y, core).
Axes of the slice: x: 4, y: 4, z: 4, core: 2. Of those that a mesh axis runs over, the one named last changes fastest.
Arguments:
- tokens: bfloat16 [16384, 2560], P(('grp', 'tok')), may hold values from -6 to 6
- input_gain: bfloat16 [2560], replicated, may hold values from 0.25 to 1.75
- query_down: bfloat16 [2560, 768], replicated, may hold values from -0.125 to 0.125
- query_gain: bfloat16 [768], replicated, may hold values from 0.25 to 1.75
- query_up: bfloat16 [768, 1920], replicated, may hold values from -0.21875 to 0.21875
- latent_down: bfloat16 [2560, 288], replicated, may hold values from -0.125 to 0.125
- latent_gain: bfloat16 [256], replicated, may hold values from 0.25 to 1.75
- key_up: bfloat16 [256, 1280], replicated, may hold values from -0.375 to 0.375
- value_up: bfloat16 [256, 1280], replicated, may hold values from -0.375 to 0.375
- output_weight: bfloat16 [1280, 2560], replicated, may hold values from -0.15625 to 0.15625
- post_gain: bfloat16 [2560], replicated, may hold values from 0.25 to 1.75
- gate_weight: bfloat16 [2560, 3200], P('tok', 'grp'), may hold values from -0.125 to 0.125
- up_weight: bfloat16 [2560, 3200], P('tok', 'grp'), may hold values from -0.125 to 0.125
- down_weight: bfloat16 [3200, 2560], P('grp', 'tok'), may hold values from -0.109375 to 0.109375
- cache_latents: bfloat16 [16, 4096, 288], P('grp', 'tok'), as said below
- prompt_latents: bfloat16 [8, 1024, 288], P(None, 'tok'), as said below
- cache_len: int32 [16], replicated, may hold values from 1 to 4096, 32768 in all
- prompt_len: int32 [8], replicated, may hold values from 1 to 1024, 4096 in all
- prompt_of: int32 [16], replicated, may hold values from 0 to 7
Outputs:
- layer_out: bfloat16 [16384, 2560], P(('grp', 'tok'))
- new_latents: bfloat16 [16384, 288], P(('grp', 'tok'))
Inputs may be any that keep to these rules, and one draw needn't show every extreme that they name: `cache_len`: some request has exactly 4096 live cached rows. `prompt_len`: some stored prompt has exactly 1024 live rows. `cache_latents`: rows past a request's live length are stored but never read. `prompt_latents`: rows past a prompt's live length are stored but never read.
All inputs are finite; a program needn't handle non-finite values.
Results may differ from a plain program's by a relative error of at most 0.02.
Values may be sent and summed in bfloat16 or wider, within the bound.
No kernel may reach another device: no remote copies, remote signals or barrier semaphores. Data moves between devices by JAX's collectives and lax.ppermute only.
A program may use at most 128 MiB of HBM per device.

v0:
```python
import jax
import jax.numpy as jnp
from jax import lax
from jax.sharding import PartitionSpec as P

KVR = 256
HEADS = 20
NOPE = 64
ROPE = 32
VDIM = 64
SPAN = 1024
EPSILON = 1e-06


def passed_along(block, axis, distance):
    devices = range(lax.axis_size(axis))
    route = [(i - distance, i) for i in devices if i - distance in devices]
    return lax.ppermute(block, axis, route)


def norm_rows(values, gain_vector):
    mean_square = jnp.mean(values * values, axis=-1, keepdims=True)
    return values * lax.rsqrt(mean_square + EPSILON) * gain_vector.astype(jnp.float32)


def rotate(values, positions):
    half_width = values.shape[-1] // 2
    frequency = 10000.0 ** (-jnp.arange(half_width, dtype=jnp.float32) / half_width)
    angles = positions.astype(jnp.float32)[:, None] * frequency[None, :]
    if values.ndim == 3:
        angles = angles[:, None, :]
    cosine = jnp.cos(angles)
    sine_part = jnp.sin(angles)
    leading = values[..., :half_width]
    trailing = values[..., half_width:]
    return jnp.concatenate(
        [leading * cosine - trailing * sine_part, trailing * cosine + leading * sine_part], axis=-1
    )


def attend_segment(
    softmax_state, queries, key_rows, lowers, limits, block_count, key_block, score_scale
):

    def fold_block(step_index, carried):
        running_max, running_sum, running_out = carried
        first_key = step_index * key_block
        key_piece = lax.dynamic_slice_in_dim(key_rows, first_key, key_block, 0)
        scores = (
            jnp.einsum("rw,kw->rk", queries, key_piece, preferred_element_type=jnp.float32)
            * score_scale
        )
        key_place = (first_key + jnp.arange(key_block, dtype=jnp.int32))[None, :]
        live_keys = jnp.logical_and(key_place >= lowers[:, None], key_place < limits[:, None])
        next_max = jnp.maximum(running_max, jnp.max(jnp.where(live_keys, scores, -1e30), axis=1))
        weights = jnp.where(live_keys, jnp.exp(scores - next_max[:, None]), 0.0)
        factor = jnp.exp(running_max - next_max)
        running_sum = running_sum * factor + jnp.sum(weights, axis=1)
        running_out = running_out * factor[:, None] + jnp.dot(
            weights.astype(jnp.bfloat16), key_piece[:, :KVR], preferred_element_type=jnp.float32
        )
        return (next_max, running_sum, running_out)

    return lax.fori_loop(0, block_count, fold_block, softmax_state)


def body(
    tokens,
    input_gain,
    query_down,
    query_gain,
    query_up,
    latent_down,
    latent_gain,
    key_up,
    value_up,
    output_weight,
    post_gain,
    gate_weight,
    up_weight,
    down_weight,
    cache_latents,
    prompt_latents,
    cache_len,
    prompt_len,
    prompt_of,
):
    group_index = lax.axis_index("grp")
    shard_index = lax.axis_index("tok")
    tok_dev = tokens.shape[0]
    tok_count = lax.axis_size("tok")
    group_requests = tok_dev * tok_count // SPAN
    local_request = shard_index % group_requests
    owner = group_index * group_requests + local_request
    offset = shard_index // group_requests * tok_dev
    within = offset + jnp.arange(tok_dev, dtype=jnp.int32)
    own_prompt = prompt_of[owner]
    prompt_live = prompt_len[own_prompt]
    cache_live = cache_len[owner]
    positions = prompt_live + cache_live + within
    normed = norm_rows(tokens.astype(jnp.float32), input_gain).astype(jnp.bfloat16)
    query_latent = norm_rows(
        jnp.dot(normed, query_down, preferred_element_type=jnp.float32), query_gain
    ).astype(jnp.bfloat16)
    query_full = jnp.dot(query_latent, query_up, preferred_element_type=jnp.float32).astype(
        jnp.bfloat16
    )
    query_full = lax.optimization_barrier(query_full).reshape(tok_dev, HEADS, NOPE + ROPE)
    absorbed = jnp.einsum(
        "thd,khd->thk",
        query_full[..., :NOPE],
        key_up.reshape(KVR, HEADS, NOPE),
        preferred_element_type=jnp.float32,
    )
    turned = rotate(query_full[..., NOPE:].astype(jnp.float32), positions)
    queries = jnp.concatenate([absorbed, turned], axis=-1).astype(jnp.bfloat16)
    latent_raw = jnp.dot(normed, latent_down, preferred_element_type=jnp.float32)
    new_latents = jnp.concatenate(
        [norm_rows(latent_raw[:, :KVR], latent_gain), rotate(latent_raw[:, KVR:], positions)],
        axis=-1,
    ).astype(jnp.bfloat16)
    latent_width = new_latents.shape[1]
    shards_back = SPAN // tok_dev
    earlier_pieces = []
    passing = new_latents
    for back in range(1, shards_back):
        passing = passed_along(passing, "tok", group_requests)
        earlier_pieces.insert(0, passing)
    span_rows = jnp.concatenate(earlier_pieces + [new_latents], axis=0)
    lead_rows = (shards_back - 1) * tok_dev
    span_lower = jnp.broadcast_to(lead_rows - offset, (tok_dev,))
    span_limit = lead_rows + 1 + jnp.arange(tok_dev, dtype=jnp.int32)
    cache_all, prompt_all = (
        lax.all_gather(cache_latents, "tok", axis=1, tiled=True),
        lax.all_gather(prompt_latents, "tok", axis=1, tiled=True),
    )
    cache_rows = lax.dynamic_index_in_dim(cache_all, local_request, 0, keepdims=False)
    prompt_rows = lax.dynamic_index_in_dim(prompt_all, own_prompt, 0, keepdims=False)
    query_rows = queries.reshape(tok_dev * HEADS, latent_width)
    row_count = tok_dev * HEADS
    score_scale = 1.0 / (NOPE + ROPE) ** 0.5
    softmax_state = (
        jnp.full((row_count,), -1e30, jnp.float32),
        jnp.zeros((row_count,), jnp.float32),
        jnp.zeros((row_count, KVR), jnp.float32),
    )
    no_lower = jnp.zeros((tok_dev,), jnp.int32)
    segments = (
        (prompt_rows, no_lower, jnp.broadcast_to(prompt_live, (tok_dev,))),
        (cache_rows, no_lower, jnp.broadcast_to(cache_live, (tok_dev,))),
        (span_rows, span_lower, span_limit),
    )
    for key_rows, token_lower, token_limit in segments:
        lowers = jnp.repeat(token_lower, HEADS)
        limits = jnp.repeat(token_limit, HEADS)
        key_block = min(512, key_rows.shape[0])
        block_count = key_rows.shape[0] // key_block
        softmax_state = attend_segment(
            softmax_state, query_rows, key_rows, lowers, limits, block_count, key_block, score_scale
        )
    running_max, running_sum, running_out = softmax_state
    latent_out = (
        (running_out / running_sum[:, None]).astype(jnp.bfloat16).reshape(tok_dev, HEADS, KVR)
    )
    heads_out = (
        jnp.einsum(
            "thk,khv->thv",
            latent_out,
            value_up.reshape(KVR, HEADS, VDIM),
            preferred_element_type=jnp.float32,
        )
        .astype(jnp.bfloat16)
        .reshape(tok_dev, HEADS * VDIM)
    )
    attended = jnp.dot(heads_out, output_weight, preferred_element_type=jnp.float32)
    residual = lax.optimization_barrier(
        (tokens.astype(jnp.float32) + attended).astype(jnp.bfloat16)
    )
    post_norm = norm_rows(residual.astype(jnp.float32), post_gain).astype(jnp.bfloat16)
    rows_all = lax.all_gather(post_norm, "grp", axis=0, tiled=True)
    gate_values = jnp.dot(
        rows_all,
        lax.all_gather(gate_weight, "tok", axis=0, tiled=True),
        preferred_element_type=jnp.float32,
    )
    up_values = jnp.dot(
        rows_all,
        lax.all_gather(up_weight, "tok", axis=0, tiled=True),
        preferred_element_type=jnp.float32,
    )
    hidden = (jax.nn.silu(gate_values) * up_values).astype(jnp.bfloat16)
    partial_out = jnp.dot(
        hidden,
        lax.all_gather(down_weight, "tok", axis=1, tiled=True),
        preferred_element_type=jnp.float32,
    )
    down_values = lax.psum_scatter(
        partial_out.astype(jnp.bfloat16), "grp", scatter_dimension=0, tiled=True
    ).astype(jnp.float32)
    layer_out = (residual.astype(jnp.float32) + down_values).astype(jnp.bfloat16)
    return (layer_out, new_latents)


def solution(mesh):
    in_specs = (
        P(("grp", "tok"), None),
        P(),
        P(),
        P(),
        P(),
        P(),
        P(),
        P(),
        P(),
        P(),
        P(),
        P("tok", "grp"),
        P("tok", "grp"),
        P("grp", "tok"),
        P("grp", "tok", None),
        P(None, "tok", None),
        P(),
        P(),
        P(),
    )
    out_specs = (P(("grp", "tok"), None), P(("grp", "tok"), None))
    return jax.shard_map(body, mesh=mesh, in_specs=in_specs, out_specs=out_specs, check_vma=False)
```

profile of v0, /device:TPU:1, one launch (start us, length us, event | category | flops | bytes accessed | tf_op | source)
XLA Modules:
  0.0 412.8 jit_solution(16430526760427926107)
XLA Ops:
  20.9 6.3 %collective-permute-start = (bf16[128,288]{0,1:T(8,128)(2,1)S(1)}, bf16[128,288]{0,1:T(8,128)(2,1)}, u32[]{:S(2)}, u32[]{:S(2)}) collective-permute-start(bf16[128,288]{0,1:T(8,128)(2,1)S(1)} %pad_maximum_fusion.1), channel_id=1, source_target_pairs={{0,4},{1,5},{2,6},{3,7},{4,8},{5,9},{6,10},{7,11},{8,12},{9,13},{1... | collective-permute-start | bytes 221192 | tf_op jit(solution)/shard_map/ppermute | solution.py:18
  27.2 3.2 multiply_reduce_fusion
  30.4 3.7 collective-permute-start.1
  36.4 4.5 %collective-permute-start.2 = (bf16[128,288]{0,1:T(8,128)(2,1)}, bf16[128,288]{0,1:T(8,128)(2,1)S(1)}, u32[]{:S(2)}, u32[]{:S(2)}) collective-permute-start(bf16[128,288]{0,1:T(8,128)(2,1)} %collective-permute-done.1), channel_id=1, source_target_pairs={{0,4},{1,5},{2,6},{3,7},{4,8},{5,9},{6,10},{7,11},{8,12},{9,13},{1... | collective-permute-start | bytes 221192 | tf_op jit(solution)/shard_map/ppermute | solution.py:18
  42.6 5.1 %collective-permute-start.3 = (bf16[128,288]{0,1:T(8,128)(2,1)S(1)}, bf16[128,288]{0,1:T(8,128)(2,1)S(1)}, u32[]{:S(2)}, u32[]{:S(2)}) collective-permute-start(bf16[128,288]{0,1:T(8,128)(2,1)S(1)} %collective-permute-done.2), channel_id=1, source_target_pairs={{0,4},{1,5},{2,6},{3,7},{4,8},{5,9},{6,10},{7,11},{8,12},{9,13},{1... | collective-permute-start | bytes 221192 | tf_op jit(solution)/shard_map/ppermute | solution.py:18
  47.7 2.9 collective-permute-done.3
  50.7 5.6 %collective-permute-start.4 = (bf16[128,288]{0,1:T(8,128)(2,1)S(1)}, bf16[128,288]{0,1:T(8,128)(2,1)S(1)}, u32[]{:S(2)}, u32[]{:S(2)}) collective-permute-start(bf16[128,288]{0,1:T(8,128)(2,1)S(1)} %collective-permute-done.3), channel_id=1, source_target_pairs={{0,4},{1,5},{2,6},{3,7},{4,8},{5,9},{6,10},{7,11},{8,12},{9,13},{1... | collective-permute-start | bytes 221192 | tf_op jit(solution)/shard_map/ppermute | solution.py:18
  62.0 6.0 %collective-permute-start.5 = (bf16[128,288]{0,1:T(8,128)(2,1)S(1)}, bf16[128,288]{0,1:T(8,128)(2,1)S(1)}, u32[]{:S(2)}, u32[]{:S(2)}) collective-permute-start(bf16[128,288]{0,1:T(8,128)(2,1)S(1)} %collective-permute-done.4), channel_id=1, source_target_pairs={{0,4},{1,5},{2,6},{3,7},{4,8},{5,9},{6,10},{7,11},{8,12},{9,13},{1... | collective-permute-start | bytes 221192 | tf_op jit(solution)/shard_map/ppermute | solution.py:18
  67.9 3.0 pad_maximum_fusion
  73.1 3.4 collective-permute-start.6
  87.5 26.8 %while.56 = (s32[]{:T(128)}, f32[2560]{0:T(1024)S(1)}, f32[2560]{0:T(1024)S(1)}, f32[2560,256]{1,0:T(8,128)S(1)}, bf16[1024,288]{1,0:T(8,128)(2,1)}, /*index=5*/...) while((s32[]{:T(128)}, f32[2560]{0:T(1024)S(1)}, ...), condition=%wide.region_5.6_spmd.clone, body=%wide.region_2.5_spmd.clone.sunk | while | flops 1439840768 | bytes 44730576 | solution.py:64
  88.0 5.6 %fusion.130 = (f32[2560]{0:T(1024)S(1)}, f32[512,2560]{1,0:T(8,128)}) fusion(pred[512]{0:T(512)(128)(4,1)S(1)} %fusion.129, bf16[2560,288]{1,0:T(8,128)(2,1)} %get-tuple-element.733, bf16[1024,288]{1,0:T(8,128)(2,1)} %get-tuple-element.732, s32[]{:T(128)S(6)} %select_n.152), kind=kOutput, calls=%fused_computation.53.clone.1 | convolution fusion | flops 758904320 | bytes 7612932 | tf_op jit(solution)/shard_map/while/body/eval_jaxpr/rw,kw->rk/dot_general | solution.py:50
  93.6 3.5 fusion.131
  97.7 2.9 convolution_add_fusion.9
  101.1 5.6 %fusion.130 = (f32[2560]{0:T(1024)S(1)}, f32[512,2560]{1,0:T(8,128)}) fusion(pred[512]{0:T(512)(128)(4,1)S(1)} %fusion.129, bf16[2560,288]{1,0:T(8,128)(2,1)} %get-tuple-element.733, bf16[1024,288]{1,0:T(8,128)(2,1)} %get-tuple-element.732, s32[]{:T(128)S(6)} %select_n.152), kind=kOutput, calls=%fused_computation.53.clone.1 | convolution fusion | flops 758904320 | bytes 7612932 | tf_op jit(solution)/shard_map/while/body/eval_jaxpr/rw,kw->rk/dot_general | solution.py:50
  106.8 3.5 fusion.131
  111.4 2.9 convolution_add_fusion.9
  114.3 14.3 %all-gather.9.cloned.1.call-done = bf16[4,4096,288]{1,2,0:T(8,128)(2,1)} async-done(((bf16[4,128,288]{1,2,0:T(8,128)(2,1)}), bf16[4,4096,288]{1,2,0:T(8,128)(2,1)}) %all-gather.9.cloned.1.call-update) | async-done | bytes 9437200 | tf_op jit(solution)/shard_map/all_gather | solution.py:134
  128.6 3.3 constant_dynamic-slice_fusion
  131.9 4.5 %copy.36 = bf16[1,4096,288]{2,1,0:T(8,128)(2,1)} copy(bf16[1,4096,288]{1,2,0:T(8,128)(2,1)} %constant_dynamic-slice_fusion) | data formatting | bytes 4718592 | tf_op jit(solution)/shard_map/jit(dynamic_index_in_dim)/dynamic_slice | solution.py:137
  136.4 61.9 %while.54 = (s32[]{:T(128)}, f32[2560]{0:T(1024)S(1)}, f32[2560]{0:T(1024)S(1)}, f32[2560,256]{1,0:T(8,128)S(1)}, bf16[4096,288]{1,0:T(8,128)(2,1)}, /*index=5*/...) while((s32[]{:T(128)}, f32[2560]{0:T(1024)S(1)}, ...), condition=%wide.region_9.10_spmd.clone, body=%wide.region_6.9_spmd.clone.sunk | while | flops 1439177728 | bytes 23759020 | solution.py:64
  137.0 3.3 fusion.119
  141.4 2.7 convolution_add_fusion.7
  144.7 3.3 fusion.119
  149.1 2.7 convolution_add_fusion.7
  152.5 3.3 fusion.119
  156.9 2.7 convolution_add_fusion.7
  160.2 3.3 fusion.119
  164.6 2.7 convolution_add_fusion.7
  167.9 3.4 fusion.119
  172.4 2.7 convolution_add_fusion.7
  175.7 3.3 fusion.119
  180.1 2.7 convolution_add_fusion.7
  183.5 3.3 fusion.119
  187.8 2.7 convolution_add_fusion.7
  191.2 3.3 fusion.119
  198.3 19.1 %while.55 = (s32[]{:T(128)}, f32[2560]{0:T(1024)S(1)}, f32[2560]{0:T(1024)S(1)}, f32[2560,256]{1,0:T(8,128)S(1)}, bf16[1024,288]{0,1:T(8,128)(2,1)}, /*index=5*/...) while((s32[]{:T(128)}, f32[2560]{0:T(1024)S(1)}, ...), condition=%wide.region_14.15_spmd.clone, body=%wide.region_11.14_spmd.clone.sunk | while | flops 1447041536 | bytes 23730872 | solution.py:64
  198.7 4.0 fusion.124
  204.6 3.3 convolution_add_fusion.8
  208.2 4.0 fusion.124
  214.1 3.3 convolution_add_fusion.8
  221.9 3.9 fusion.59
  228.6 32.8 %all-gather.11.cloned.1.call-done = bf16[512,2560]{1,0:T(8,128)(2,1)} async-done(((bf16[128,2560]{1,0:T(8,128)(2,1)}), bf16[512,2560]{1,0:T(8,128)(2,1)}) %all-gather.11.cloned.1.call-update) | async-done | bytes 2621456 | tf_op jit(solution)/shard_map/all_gather | solution.py:180
  261.4 6.7 %fusion.81 = f32[512,800]{0,1:T(8,128)} fusion(bf16[512,2560]{1,0:T(8,128)(2,1)} %all-gather.11.cloned.1.call-done, bf16[2560,800]{1,0:T(8,128)(2,1)} %all-gather.13.cloned.1.call-done), kind=kOutput, calls=%fused_computation.136 | convolution fusion | flops 2097152000 | bytes 8355840 | tf_op jit(solution)/shard_map/dot_general | solution.py:181
  268.1 42.8 %all-gather.15.cloned.1.call-done = bf16[2560,800]{1,0:T(8,128)(2,1)} async-done(((bf16[80,800]{1,0:T(8,128)(2,1)}), bf16[2560,800]{1,0:T(8,128)(2,1)}) %all-gather.15.cloned.1.call-update) | async-done | bytes 4096016 | tf_op jit(solution)/shard_map/all_gather | solution.py:188
  310.9 48.1 %all-gather.17.cloned.1.call-done = bf16[800,2560]{0,1:T(8,128)(2,1)} async-done(((bf16[800,80]{0,1:T(8,128)(2,1)}), bf16[800,2560]{0,1:T(8,128)(2,1)}) %all-gather.17.cloned.1.call-update) | async-done | bytes 4096016 | tf_op jit(solution)/shard_map/all_gather | solution.py:194
  358.9 11.8 %convolution_convert_fusion = bf16[512,2560]{1,0:T(8,128)(2,1)} fusion(bf16[800,2560]{0,1:T(8,128)(2,1)} %all-gather.17.cloned.1.call-done, f32[512,800]{0,1:T(8,128)} %fusion.81, bf16[512,2560]{1,0:T(8,128)(2,1)} %all-gather.11.cloned.1.call-done, bf16[2560,800]{1,0:T(8,128)(2,1)} %all-gather.15.cloned.1.call-done), kind=kOutput, calls=%fused_computation.77 | convolution fusion | flops 4198072320 | bytes 15073280 | tf_op jit(solution)/shard_map/dot_general | solution.py:192
  370.7 32.9 %reduce-scatter.2.cloned.1.call-done = bf16[128,2560]{1,0:T(8,128)(2,1)} async-done(((bf16[512,2560]{1,0:T(8,128)(2,1)}), bf16[128,2560]{1,0:T(8,128)(2,1)}) %reduce-scatter.2.cloned.1.call-update) | async-done | bytes 655376 | tf_op jit(solution)/shard_map/reduce_scatter | solution.py:197
  (160 shorter events, 65.5 us)
Async XLA Ops:
  7.2 26.9 %copy-start = (bf16[768,1920]{1,0:T(8,128)(2,1)S(1)}, bf16[768,1920]{1,0:T(8,128)(2,1)}, u32[]{:S(2)}) copy-start(bf16[768,1920]{1,0:T(8,128)(2,1)} %param.29) | copy-start | bytes 8847364
  7.2 78.2 %all-gather.7.cloned.1.call-start = ((), (), s32[]{:S(2)}) async-start(), calls=%async_computation.1 | async-start | bytes 6488064 | tf_op jit(solution)/shard_map/all_gather | solution.py:135
  7.9 120.7 %all-gather.9.cloned.1.call-start = ((), (), s32[]{:S(2)}) async-start(), calls=%async_computation.2 | async-start | bytes 9732096 | tf_op jit(solution)/shard_map/all_gather | solution.py:134
  8.7 219.9 %all-gather.13.cloned.1.call-start = ((), (), s32[]{:S(2)}) async-start(), calls=%async_computation.4 | async-start | bytes 4730880 | tf_op jit(solution)/shard_map/all_gather | solution.py:183
  20.8 9.6 %copy-start.8 = (bf16[768]{0:T(1024)(128)(2,1)S(1)}, bf16[768]{0:T(1024)(128)(2,1)}, u32[]{:S(2)}) copy-start(bf16[768]{0:T(1024)(128)(2,1)} %param.28) | copy-start | bytes 4612
  20.8 13.3 %copy-start.6 = (bf16[128,288]{0,1:T(8,128)(2,1)}, bf16[128,288]{0,1:T(8,128)(2,1)S(1)}, u32[]{:S(2)}) copy-start(bf16[128,288]{0,1:T(8,128)(2,1)S(1)} %pad_maximum_fusion.1) | copy-start | bytes 221188
  20.9 9.6 %collective-permute-start = (bf16[128,288]{0,1:T(8,128)(2,1)S(1)}, bf16[128,288]{0,1:T(8,128)(2,1)}, u32[]{:S(2)}, u32[]{:S(2)}) collective-permute-start(bf16[128,288]{0,1:T(8,128)(2,1)S(1)} %pad_maximum_fusion.1), channel_id=1, source_target_pairs={{0,4},{1,5},{2,6},{3,7},{4,8},{5,9},{6,10},{7,11},{8,12},{9,13},{1... | collective-permute-start | bytes 221192 | tf_op jit(solution)/shard_map/ppermute | solution.py:18
  27.1 234.2 %all-gather.11.cloned.1.call-start = ((), (), s32[]{:S(2)}) async-start(), calls=%async_computation.3 | async-start | bytes 3276800 | tf_op jit(solution)/shard_map/all_gather | solution.py:180
  30.4 5.9 %collective-permute-start.1 = (bf16[128,288]{0,1:T(8,128)(2,1)}, bf16[128,288]{0,1:T(8,128)(2,1)}, u32[]{:S(2)}, u32[]{:S(2)}) collective-permute-start(bf16[128,288]{0,1:T(8,128)(2,1)} %collective-permute-done), channel_id=1, source_target_pairs={{0,4},{1,5},{2,6},{3,7},{4,8},{5,9},{6,10},{7,11},{8,12},{9,13},{1... | collective-permute-start | bytes 221192 | tf_op jit(solution)/shard_map/ppermute | solution.py:18
  36.4 6.2 %collective-permute-start.2 = (bf16[128,288]{0,1:T(8,128)(2,1)}, bf16[128,288]{0,1:T(8,128)(2,1)S(1)}, u32[]{:S(2)}, u32[]{:S(2)}) collective-permute-start(bf16[128,288]{0,1:T(8,128)(2,1)} %collective-permute-done.1), channel_id=1, source_target_pairs={{0,4},{1,5},{2,6},{3,7},{4,8},{5,9},{6,10},{7,11},{8,12},{9,13},{1... | collective-permute-start | bytes 221192 | tf_op jit(solution)/shard_map/ppermute | solution.py:18
  42.6 8.1 %collective-permute-start.3 = (bf16[128,288]{0,1:T(8,128)(2,1)S(1)}, bf16[128,288]{0,1:T(8,128)(2,1)S(1)}, u32[]{:S(2)}, u32[]{:S(2)}) collective-permute-start(bf16[128,288]{0,1:T(8,128)(2,1)S(1)} %collective-permute-done.2), channel_id=1, source_target_pairs={{0,4},{1,5},{2,6},{3,7},{4,8},{5,9},{6,10},{7,11},{8,12},{9,13},{1... | collective-permute-start | bytes 221192 | tf_op jit(solution)/shard_map/ppermute | solution.py:18
  50.7 11.3 %collective-permute-start.4 = (bf16[128,288]{0,1:T(8,128)(2,1)S(1)}, bf16[128,288]{0,1:T(8,128)(2,1)S(1)}, u32[]{:S(2)}, u32[]{:S(2)}) collective-permute-start(bf16[128,288]{0,1:T(8,128)(2,1)S(1)} %collective-permute-done.3), channel_id=1, source_target_pairs={{0,4},{1,5},{2,6},{3,7},{4,8},{5,9},{6,10},{7,11},{8,12},{9,13},{1... | collective-permute-start | bytes 221192 | tf_op jit(solution)/shard_map/ppermute | solution.py:18
  62.0 11.2 %copy-start.7 = (bf16[2560]{0:T(1024)(128)(2,1)S(1)}, bf16[2560]{0:T(1024)(128)(2,1)}, u32[]{:S(2)}) copy-start(bf16[2560]{0:T(1024)(128)(2,1)} %param.35) | copy-start | bytes 15364
  62.0 11.2 %collective-permute-start.5 = (bf16[128,288]{0,1:T(8,128)(2,1)S(1)}, bf16[128,288]{0,1:T(8,128)(2,1)S(1)}, u32[]{:S(2)}, u32[]{:S(2)}) collective-permute-start(bf16[128,288]{0,1:T(8,128)(2,1)S(1)} %collective-permute-done.4), channel_id=1, source_target_pairs={{0,4},{1,5},{2,6},{3,7},{4,8},{5,9},{6,10},{7,11},{8,12},{9,13},{1... | collective-permute-start | bytes 221192 | tf_op jit(solution)/shard_map/ppermute | solution.py:18
  73.1 5.2 %collective-permute-start.6 = (bf16[128,288]{0,1:T(8,128)(2,1)S(1)}, bf16[128,288]{0,1:T(8,128)(2,1)S(1)}, u32[]{:S(2)}, u32[]{:S(2)}) collective-permute-start(bf16[128,288]{0,1:T(8,128)(2,1)S(1)} %collective-permute-done.5), channel_id=1, source_target_pairs={{0,4},{1,5},{2,6},{3,7},{4,8},{5,9},{6,10},{7,11},{8,12},{9,13},{1... | collective-permute-start | bytes 221192 | tf_op jit(solution)/shard_map/ppermute | solution.py:18
  93.6 4.0 copy-start.2
  106.8 4.7 %copy-start.2 = (f32[512,2560]{1,0:T(8,128)S(1)}, f32[512,2560]{1,0:T(8,128)}, u32[]{:S(2)}) copy-start(f32[512,2560]{1,0:T(8,128)} %get-tuple-element.703) | copy-start | bytes 15728644 | tf_op jit(solution)/shard_map/while
  218.9 2.3 copy-start.5
  218.9 2.9 copy-start.4
  225.8 42.3 %copy-start.3 = (bf16[128,2560]{1,0:T(8,128)(2,1)}, bf16[128,2560]{1,0:T(8,128)(2,1)S(1)}, u32[]{:S(2)}) copy-start(bf16[128,2560]{1,0:T(8,128)(2,1)S(1)} %fusion.59) | copy-start | bytes 1966084
  227.1 83.7 %all-gather.15.cloned.1.call-start = ((), (), s32[]{:S(2)}) async-start(), calls=%async_computation.5 | async-start | bytes 4730880 | tf_op jit(solution)/shard_map/all_gather | solution.py:188
  227.7 131.2 %all-gather.17.cloned.1.call-start = ((), (), s32[]{:S(2)}) async-start(), calls=%async_computation.6 | async-start | bytes 4730880 | tf_op jit(solution)/shard_map/all_gather | solution.py:194
  228.3 175.4 %reduce-scatter.2.cloned.1.call-start = ((), (), s32[]{:S(2)}) async-start(), calls=%async_computation.7 | async-start | bytes 3276800 | tf_op jit(solution)/shard_map/reduce_scatter | solution.py:197
  358.9 47.0 %copy-start.1 = (bf16[768,1920]{1,0:T(8,128)(2,1)S(1)}, bf16[768,1920]{1,0:T(8,128)(2,1)}, u32[]{:S(2)}) copy-start(bf16[768,1920]{1,0:T(8,128)(2,1)} %param.29) | copy-start | bytes 8847364
Sparse Core Ops, SparseCore 0:
  10.3 55.2 all-gather.6
  67.7 60.8 all-gather.8
  130.9 46.1 all-gather.12
  227.2 34.1 all-gather.10
  263.6 47.2 all-gather.14
  313.0 45.8 all-gather.16
  370.9 32.7 reduce-scatter.1
where the time goes:
time: 415 us; the launch traced here: 413 us
  waiting for transfers between devices  179 us (43%)
  matrix products  109 us (26%)
  other arithmetic  37.2 us (9%)
  starting transfers between devices  35.1 us (8%)
  local copies, waits for them, and re-layouts  33.7 us (8%)
  between operations  17.6 us (4%)
    all_gather x1, waiting for transfers between devices, body(): lax.all_gather(down_weight, 'tok', axis=1, tiled=True)  48.1 us
    dot_general x12, matrix products, fold_block(): jnp.einsum('rw,kw->rk', queries, key_piece, preferred_element_type=jnp.fl...  45.9 us
    all_gather x1, waiting for transfers between devices, body(): lax.all_gather(up_weight, 'tok', axis=0, tiled=True)  42.8 us
    ppermute x7, starting transfers between devices, passed_along(): return lax.ppermute(block, axis, route)  34.6 us
    dot_general x12, matrix products, fold_block(): jnp.dot(weights.astype(jnp.bfloat16), key_piece[:, :KVR], preferred_eleme...  33.7 us
    reduce_scatter x1, waiting for transfers between devices, body(): lax.psum_scatter(partial_out.astype(jnp.bfloat16), 'grp', scatter_dimensi...  32.9 us
    all_gather x1, waiting for transfers between devices, body(): rows_all = lax.all_gather(post_norm, 'grp', axis=0, tiled=True)  32.8 us
    reduce_sum x12, other arithmetic, fold_block(): running_sum = running_sum * factor + jnp.sum(weights, axis=1)  19 us
  transfers between devices with their start and end apart: 14, of which 8 were waited for; matrix products, arithmetic and copies ran while one was open for 40% of the time, Pallas kernels for 0%

commit v1 on v0

--- a/solution.py
+++ b/solution.py
@@ -10,6 +10,12 @@
 VDIM = 64
 SPAN = 1024
 EPSILON = 1e-06
+
+
+def produce_counts(t0):
+    group_axis = "tok"
+    low = jnp.concatenate(lax.axis_size(group_axis) * [t0], axis=1)
+    return lax.all_to_all(low, group_axis, 1, 1, tiled=True)
 
 
 def passed_along(block, axis, distance):
@@ -131,7 +137,7 @@
     span_lower = jnp.broadcast_to(lead_rows - offset, (tok_dev,))
     span_limit = lead_rows + 1 + jnp.arange(tok_dev, dtype=jnp.int32)
     cache_all, prompt_all = (
-        lax.all_gather(cache_latents, "tok", axis=1, tiled=True),
+        produce_counts(cache_latents),
         lax.all_gather(prompt_latents, "tok", axis=1, tiled=True),
     )
     cache_rows = lax.dynamic_index_in_dim(cache_all, local_request, 0, keepdims=False)

time: 415 us -> 633 us (1.53)
  waiting for transfers between devices: 179 us -> 306 us
  local copies, waits for them, and re-layouts: 33.7 us -> 99.9 us
  starting transfers between devices: 35.1 us -> 58.8 us
    ppermute x7, waiting for transfers between devices: 5.92 us -> 139 us  [passed_along(): return lax.ppermute(block, axis, route)]
    unnamed x25 -> x65, local copies, waits for them, and re-layouts: 9.84 us -> 56.6 us
    concatenate x0 -> x2, local copies, waits for them, and re-layouts: none -> 20 us  [produce_counts(): low = jnp.concatenate(lax.axis_size(group_axis) * [t0], axis=1)]
    all_gather x1 -> x0, waiting for transfers between devices: 14.3 us -> none  [body(): lax.all_gather(cache_latents, 'tok', axis=1, tiled=True)]
    ppermute x7, starting transfers between devices: 34.6 us -> 48.5 us  [passed_along(): return lax.ppermute(block, axis, route)]
    all_to_all x0 -> x1, starting transfers between devices: none -> 9.8 us  [produce_counts(): return lax.all_to_all(low, group_axis, 1, 1, tiled=True)]
    all_gather x1, waiting for transfers between devices: 32.8 us -> 40.8 us  [body(): rows_all = lax.all_gather(post_norm, 'grp', axis=0, tiled=True)]
  transfers between devices with their start and end apart: 14 -> 14, of which waited for: 8 -> 8; matrix products, arithmetic and copies ran while one was open for 40% -> 37% of each run, Pallas kernels for 0% -> 0%
where the time goes in v1:
time: 633 us; the launch traced here: 630 us
  waiting for transfers between devices  306 us (48%)
  matrix products  112 us (18%)
  local copies, waits for them, and re-layouts  99.9 us (16%)
  starting transfers between devices  58.8 us (9%)
  other arithmetic  35.3 us (6%)
  between operations  17.6 us (3%)
    ppermute x7, waiting for transfers between devices, passed_along(): return lax.ppermute(block, axis, route)  139 us
    unnamed x65, local copies, waits for them, and re-layouts  56.6 us
    ppermute x7, starting transfers between devices, passed_along(): return lax.ppermute(block, axis, route)  48.5 us
    all_gather x1, waiting for transfers between devices, body(): lax.all_gather(down_weight, 'tok', axis=1, tiled=True)  48 us
    dot_general x12, matrix products, fold_block(): jnp.einsum('rw,kw->rk', queries, key_piece, preferred_element_type=jnp.fl...  47.2 us
    all_gather x1, waiting for transfers between devices, body(): lax.all_gather(up_weight, 'tok', axis=0, tiled=True)  42.8 us
    all_gather x1, waiting for transfers between devices, body(): rows_all = lax.all_gather(post_norm, 'grp', axis=0, tiled=True)  40.8 us
    dot_general x12, matrix products, fold_block(): jnp.dot(weights.astype(jnp.bfloat16), key_piece[:, :KVR], preferred_eleme...  33.7 us
  transfers between devices with their start and end apart: 14, of which 8 were waited for; matrix products, arithmetic and copies ran while one was open for 37% of the time, Pallas kernels for 0%

profile of v1, /device:TPU:1, one launch (start us, length us, event | category | flops | bytes accessed | tf_op | source)
XLA Modules:
  0.0 630.0 jit_solution(3551513141823834616)
XLA Ops:
  41.6 19.2 %copy.133 = bf16[4,4096,288]{2,0,1:T(4,128)(2,1)} copy(bf16[4,4096,288]{1,2,0:T(8,128)(2,1)} %constant_dynamic-update-slice_fusion) | data formatting | bytes 18874368 | tf_op jit(solution)/shard_map/concatenate | solution.py:17
  60.8 9.8 %all-to-all-start = ((bf16[4,4096,288]{2,0,1:T(4,128)(2,1)}), bf16[4,4096,288]{2,0,1:T(4,128)(2,1)}, u32[]{:S(2)}, u32[]{:S(2)}) async-start(bf16[4,4096,288]{2,0,1:T(4,128)(2,1)} %copy.133), calls=%async_computation | async-start | bytes 25165824 | tf_op jit(solution)/shard_map/all_to_all | solution.py:18
  79.5 5.4 collective-permute-start
  85.0 3.1 multiply_reduce_fusion
  88.1 135.7 %collective-permute-done = bf16[128,288]{0,1:T(8,128)(2,1)} collective-permute-done((bf16[128,288]{0,1:T(8,128)(2,1)S(1)}, bf16[128,288]{0,1:T(8,128)(2,1)}, u32[]{:S(2)}, u32[]{:S(2)}) %collective-permute-start) | collective-permute-done | bytes 73760 | tf_op jit(solution)/shard_map/ppermute | solution.py:24
  223.9 10.0 %collective-permute-start.1 = (bf16[128,288]{0,1:T(8,128)(2,1)}, bf16[128,288]{0,1:T(8,128)(2,1)}, u32[]{:S(2)}, u32[]{:S(2)}) collective-permute-start(bf16[128,288]{0,1:T(8,128)(2,1)} %collective-permute-done), channel_id=1, source_target_pairs={{0,4},{1,5},{2,6},{3,7},{4,8},{5,9},{6,10},{7,11},{8,12},{9,13},{1... | collective-permute-start | bytes 221192 | tf_op jit(solution)/shard_map/ppermute | solution.py:24
  236.1 6.0 collective-permute-start.2
  243.9 8.8 %collective-permute-start.3 = (bf16[128,288]{0,1:T(8,128)(2,1)S(1)}, bf16[128,288]{0,1:T(8,128)(2,1)S(1)}, u32[]{:S(2)}, u32[]{:S(2)}) collective-permute-start(bf16[128,288]{0,1:T(8,128)(2,1)S(1)} %collective-permute-done.2), channel_id=1, source_target_pairs={{0,4},{1,5},{2,6},{3,7},{4,8},{5,9},{6,10},{7,11},{8,12},{9,13},{1... | collective-permute-start | bytes 221192 | tf_op jit(solution)/shard_map/ppermute | solution.py:24
  254.1 6.6 %collective-permute-start.4 = (bf16[128,288]{0,1:T(8,128)(2,1)S(1)}, bf16[128,288]{0,1:T(8,128)(2,1)S(1)}, u32[]{:S(2)}, u32[]{:S(2)}) collective-permute-start(bf16[128,288]{0,1:T(8,128)(2,1)S(1)} %collective-permute-done.3), channel_id=1, source_target_pairs={{0,4},{1,5},{2,6},{3,7},{4,8},{5,9},{6,10},{7,11},{8,12},{9,13},{1... | collective-permute-start | bytes 221192 | tf_op jit(solution)/shard_map/ppermute | solution.py:24
  266.3 6.1 collective-permute-start.5
  272.5 3.0 pad_maximum_fusion
  277.6 5.6 collective-permute-start.6
  291.4 10.1 %constant_dynamic-slice_fusion = bf16[1,4096,288]{2,0,1:T(2,128)(2,1)} fusion(bf16[4,4096,288]{2,0,1:T(4,128)(2,1)} %all-to-all-done, s32[]{:T(128)S(6)} %select_n.92), kind=kLoop, calls=%fused_computation.166 | loop fusion | bytes 4718596 | tf_op jit(solution)/shard_map/jit(dynamic_index_in_dim)/dynamic_slice | solution.py:143
  301.5 13.9 %copy.141 = bf16[1,4096,288]{1,2,0:T(8,128)(2,1)} copy(bf16[1,4096,288]{2,0,1:T(2,128)(2,1)} %constant_dynamic-slice_fusion) | data formatting | bytes 4718592
  317.4 26.3 %while.56 = (s32[]{:T(128)}, f32[2560]{0:T(1024)S(1)}, f32[2560]{0:T(1024)S(1)}, f32[2560,256]{1,0:T(8,128)S(1)}, bf16[1024,288]{1,0:T(8,128)(2,1)}, /*index=5*/...) while((s32[]{:T(128)}, f32[2560]{0:T(1024)S(1)}, ...), condition=%wide.region_5.6_spmd.clone, body=%wide.region_2.5_spmd.clone.sunk | while | flops 1439840768 | bytes 44730576 | solution.py:70
  318.1 5.6 fusion.130
  323.7 3.5 fusion.131
  327.7 2.9 convolution_add_fusion.9
  331.2 5.6 fusion.130
  336.9 3.5 fusion.131
  340.9 2.9 convolution_add_fusion.9
  343.8 62.6 %while.54 = (s32[]{:T(128)}, f32[2560]{0:T(1024)S(1)}, f32[2560]{0:T(1024)S(1)}, f32[2560,256]{1,0:T(8,128)S(1)}, bf16[4096,288]{0,1:T(8,128)(2,1)}, /*index=5*/...) while((s32[]{:T(128)}, f32[2560]{0:T(1024)S(1)}, ...), condition=%wide.region_9.10_spmd.clone, body=%wide.region_6.9_spmd.clone.sunk | while | flops 1439177728 | bytes 23660716 | solution.py:70
  344.3 3.5 fusion.119
  352.2 3.5 fusion.119
  356.7 2.7 convolution_add_fusion.7
  360.0 3.5 fusion.119
  364.5 2.7 convolution_add_fusion.7
  367.8 3.5 fusion.119
  372.4 2.7 convolution_add_fusion.7
  375.6 3.5 fusion.119
  383.5 3.5 fusion.119
  388.0 2.7 convolution_add_fusion.7
  391.3 3.5 fusion.119
  395.8 2.7 convolution_add_fusion.7
  399.1 3.5 fusion.119
  403.7 2.7 convolution_add_fusion.7
  406.4 19.1 %while.55 = (s32[]{:T(128)}, f32[2560]{0:T(1024)S(1)}, f32[2560]{0:T(1024)S(1)}, f32[2560,256]{1,0:T(8,128)S(1)}, bf16[1024,288]{0,1:T(8,128)(2,1)}, /*index=5*/...) while((s32[]{:T(128)}, f32[2560]{0:T(1024)S(1)}, ...), condition=%wide.region_14.15_spmd.clone, body=%wide.region_11.14_spmd.clone.sunk | while | flops 1447041536 | bytes 23730872 | solution.py:70
  406.8 4.0 fusion.124
  412.7 3.3 convolution_add_fusion.8
  416.3 4.0 fusion.124
  422.2 3.3 convolution_add_fusion.8
  430.9 4.0 fusion.59
  437.8 40.8 %all-gather.8.cloned.1.call-done = bf16[512,2560]{1,0:T(8,128)(2,1)} async-done(((bf16[128,2560]{1,0:T(8,128)(2,1)}), bf16[512,2560]{1,0:T(8,128)(2,1)}) %all-gather.8.cloned.1.call-update) | async-done | bytes 2621456 | tf_op jit(solution)/shard_map/all_gather | solution.py:186
  478.5 6.7 %fusion.81 = f32[512,800]{0,1:T(8,128)} fusion(bf16[512,2560]{1,0:T(8,128)(2,1)} %all-gather.8.cloned.1.call-done, bf16[2560,800]{1,0:T(8,128)(2,1)} %all-gather.10.cloned.1.call-done), kind=kOutput, calls=%fused_computation.168 | convolution fusion | flops 2097152000 | bytes 8355840 | tf_op jit(solution)/shard_map/dot_general | solution.py:187
  485.2 42.8 %all-gather.12.cloned.1.call-done = bf16[2560,800]{1,0:T(8,128)(2,1)} async-done(((bf16[80,800]{1,0:T(8,128)(2,1)}), bf16[2560,800]{1,0:T(8,128)(2,1)}) %all-gather.12.cloned.1.call-update) | async-done | bytes 4096016 | tf_op jit(solution)/shard_map/all_gather | solution.py:194
  528.0 48.0 %all-gather.14.cloned.1.call-done = bf16[800,2560]{0,1:T(8,128)(2,1)} async-done(((bf16[800,80]{0,1:T(8,128)(2,1)}), bf16[800,2560]{0,1:T(8,128)(2,1)}) %all-gather.14.cloned.1.call-update) | async-done | bytes 4096016 | tf_op jit(solution)/shard_map/all_gather | solution.py:200
  576.0 11.8 %convolution_convert_fusion = bf16[512,2560]{1,0:T(8,128)(2,1)} fusion(bf16[800,2560]{0,1:T(8,128)(2,1)} %all-gather.14.cloned.1.call-done, f32[512,800]{0,1:T(8,128)} %fusion.81, bf16[512,2560]{1,0:T(8,128)(2,1)} %all-gather.8.cloned.1.call-done, bf16[2560,800]{1,0:T(8,128)(2,1)} %all-gather.12.cloned.1.call-done), kind=kOutput, calls=%fused_computation.77 | convolution fusion | flops 4198072320 | bytes 15073280 | tf_op jit(solution)/shard_map/dot_general | solution.py:198
  587.9 32.9 %reduce-scatter.2.cloned.1.call-done = bf16[128,2560]{1,0:T(8,128)(2,1)} async-done(((bf16[512,2560]{1,0:T(8,128)(2,1)}), bf16[128,2560]{1,0:T(8,128)(2,1)}) %reduce-scatter.2.cloned.1.call-update) | async-done | bytes 655376 | tf_op jit(solution)/shard_map/reduce_scatter | solution.py:203
  (200 shorter events, 98.3 us)
Async XLA Ops:
  7.2 226.7 %copy-start = (bf16[768,1920]{1,0:T(8,128)(2,1)S(1)}, bf16[768,1920]{1,0:T(8,128)(2,1)}, u32[]{:S(2)}) copy-start(bf16[768,1920]{1,0:T(8,128)(2,1)} %param.29) | copy-start | bytes 8847364
  7.2 16.5 %copy-start.2 = (bf16[4,128,288]{1,2,0:T(8,128)(2,1)S(1)}, bf16[4,128,288]{1,2,0:T(8,128)(2,1)}, u32[]{:S(2)}) copy-start(bf16[4,128,288]{1,2,0:T(8,128)(2,1)} %param.39) | copy-start | bytes 884740
  7.2 308.1 %all-gather.6.cloned.1.call-start = ((), (), s32[]{:S(2)}) async-start(), calls=%async_computation.2 | async-start | bytes 6488064 | tf_op jit(solution)/shard_map/all_gather | solution.py:141
  60.8 9.9 %copy-start.9 = (s32[16]{0:T(128)S(1)}, s32[16]{0:T(128)}, u32[]{:S(2)}) copy-start(s32[16]{0:T(128)} %param.43) | copy-start | bytes 196
  60.8 11.8 %copy-start.10 = (s32[16]{0:T(128)S(1)}, s32[16]{0:T(128)}, u32[]{:S(2)}) copy-start(s32[16]{0:T(128)} %param.41) | copy-start | bytes 196
  60.8 12.4 %copy-start.6 = (bf16[2560]{0:T(1024)(128)(2,1)S(1)}, bf16[2560]{0:T(1024)(128)(2,1)}, u32[]{:S(2)}) copy-start(bf16[2560]{0:T(1024)(128)(2,1)} %param.26) | copy-start | bytes 15364
  60.8 12.4 %copy-start.11 = (bf16[256]{0:T(256)(128)(2,1)S(1)}, bf16[256]{0:T(256)(128)(2,1)}, u32[]{:S(2)}) copy-start(bf16[256]{0:T(256)(128)(2,1)} %param.31) | copy-start | bytes 1540
  60.8 13.0 %copy-start.12 = (s32[8]{0:T(128)S(1)}, s32[8]{0:T(128)}, u32[]{:S(2)}) copy-start(s32[8]{0:T(128)} %param.42) | copy-start | bytes 100
  60.8 230.6 %all-to-all-start = ((bf16[4,4096,288]{2,0,1:T(4,128)(2,1)}), bf16[4,4096,288]{2,0,1:T(4,128)(2,1)}, u32[]{:S(2)}, u32[]{:S(2)}) async-start(bf16[4,4096,288]{2,0,1:T(4,128)(2,1)} %copy.133), calls=%async_computation | async-start | bytes 25165824 | tf_op jit(solution)/shard_map/all_to_all | solution.py:18
  70.6 17.5 %copy-start.8 = (bf16[768]{0:T(1024)(128)(2,1)S(1)}, bf16[768]{0:T(1024)(128)(2,1)}, u32[]{:S(2)}) copy-start(bf16[768]{0:T(1024)(128)(2,1)} %param.28) | copy-start | bytes 4612
  70.6 367.1 %all-gather.10.cloned.1.call-start = ((), (), s32[]{:S(2)}) async-start(), calls=%async_computation.4 | async-start | bytes 4730880 | tf_op jit(solution)/shard_map/all_gather | solution.py:189
  79.5 154.4 %copy-start.5 = (bf16[128,288]{0,1:T(8,128)(2,1)}, bf16[128,288]{0,1:T(8,128)(2,1)S(1)}, u32[]{:S(2)}) copy-start(bf16[128,288]{0,1:T(8,128)(2,1)S(1)} %pad_maximum_fusion.1) | copy-start | bytes 221188
  79.5 144.4 %collective-permute-start = (bf16[128,288]{0,1:T(8,128)(2,1)S(1)}, bf16[128,288]{0,1:T(8,128)(2,1)}, u32[]{:S(2)}, u32[]{:S(2)}) collective-permute-start(bf16[128,288]{0,1:T(8,128)(2,1)S(1)} %pad_maximum_fusion.1), channel_id=1, source_target_pairs={{0,4},{1,5},{2,6},{3,7},{4,8},{5,9},{6,10},{7,11},{8,12},{9,13},{1... | collective-permute-start | bytes 221192 | tf_op jit(solution)/shard_map/ppermute | solution.py:24
  84.9 393.6 %all-gather.8.cloned.1.call-start = ((), (), s32[]{:S(2)}) async-start(), calls=%async_computation.3 | async-start | bytes 3276800 | tf_op jit(solution)/shard_map/all_gather | solution.py:186
  223.9 12.3 %collective-permute-start.1 = (bf16[128,288]{0,1:T(8,128)(2,1)}, bf16[128,288]{0,1:T(8,128)(2,1)}, u32[]{:S(2)}, u32[]{:S(2)}) collective-permute-start(bf16[128,288]{0,1:T(8,128)(2,1)} %collective-permute-done), channel_id=1, source_target_pairs={{0,4},{1,5},{2,6},{3,7},{4,8},{5,9},{6,10},{7,11},{8,12},{9,13},{1... | collective-permute-start | bytes 221192 | tf_op jit(solution)/shard_map/ppermute | solution.py:24
  236.1 7.7 %collective-permute-start.2 = (bf16[128,288]{0,1:T(8,128)(2,1)}, bf16[128,288]{0,1:T(8,128)(2,1)S(1)}, u32[]{:S(2)}, u32[]{:S(2)}) collective-permute-start(bf16[128,288]{0,1:T(8,128)(2,1)} %collective-permute-done.1), channel_id=1, source_target_pairs={{0,4},{1,5},{2,6},{3,7},{4,8},{5,9},{6,10},{7,11},{8,12},{9,13},{1... | collective-permute-start | bytes 221192 | tf_op jit(solution)/shard_map/ppermute | solution.py:24
  243.9 10.2 %collective-permute-start.3 = (bf16[128,288]{0,1:T(8,128)(2,1)S(1)}, bf16[128,288]{0,1:T(8,128)(2,1)S(1)}, u32[]{:S(2)}, u32[]{:S(2)}) collective-permute-start(bf16[128,288]{0,1:T(8,128)(2,1)S(1)} %collective-permute-done.2), channel_id=1, source_target_pairs={{0,4},{1,5},{2,6},{3,7},{4,8},{5,9},{6,10},{7,11},{8,12},{9,13},{1... | collective-permute-start | bytes 221192 | tf_op jit(solution)/shard_map/ppermute | solution.py:24
  254.1 12.3 %collective-permute-start.4 = (bf16[128,288]{0,1:T(8,128)(2,1)S(1)}, bf16[128,288]{0,1:T(8,128)(2,1)S(1)}, u32[]{:S(2)}, u32[]{:S(2)}) collective-permute-start(bf16[128,288]{0,1:T(8,128)(2,1)S(1)} %collective-permute-done.3), channel_id=1, source_target_pairs={{0,4},{1,5},{2,6},{3,7},{4,8},{5,9},{6,10},{7,11},{8,12},{9,13},{1... | collective-permute-start | bytes 221192 | tf_op jit(solution)/shard_map/ppermute | solution.py:24
  265.3 12.3 %copy-start.7 = (bf16[2560]{0:T(1024)(128)(2,1)S(1)}, bf16[2560]{0:T(1024)(128)(2,1)}, u32[]{:S(2)}) copy-start(bf16[2560]{0:T(1024)(128)(2,1)} %param.35) | copy-start | bytes 15364
  266.3 11.3 %collective-permute-start.5 = (bf16[128,288]{0,1:T(8,128)(2,1)S(1)}, bf16[128,288]{0,1:T(8,128)(2,1)S(1)}, u32[]{:S(2)}, u32[]{:S(2)}) collective-permute-start(bf16[128,288]{0,1:T(8,128)(2,1)S(1)} %collective-permute-done.4), channel_id=1, source_target_pairs={{0,4},{1,5},{2,6},{3,7},{4,8},{5,9},{6,10},{7,11},{8,12},{9,13},{1... | collective-permute-start | bytes 221192 | tf_op jit(solution)/shard_map/ppermute | solution.py:24
  277.6 6.8 %collective-permute-start.6 = (bf16[128,288]{0,1:T(8,128)(2,1)S(1)}, bf16[128,288]{0,1:T(8,128)(2,1)S(1)}, u32[]{:S(2)}, u32[]{:S(2)}) collective-permute-start(bf16[128,288]{0,1:T(8,128)(2,1)S(1)} %collective-permute-done.5), channel_id=1, source_target_pairs={{0,4},{1,5},{2,6},{3,7},{4,8},{5,9},{6,10},{7,11},{8,12},{9,13},{1... | collective-permute-start | bytes 221192 | tf_op jit(solution)/shard_map/ppermute | solution.py:24
  323.7 4.0 copy-start.3
  336.9 4.0 copy-start.3
  434.9 50.3 %copy-start.4 = (bf16[128,2560]{1,0:T(8,128)(2,1)}, bf16[128,2560]{1,0:T(8,128)(2,1)S(1)}, u32[]{:S(2)}) copy-start(bf16[128,2560]{1,0:T(8,128)(2,1)S(1)} %fusion.59) | copy-start | bytes 1966084
  436.3 91.7 %all-gather.12.cloned.1.call-start = ((), (), s32[]{:S(2)}) async-start(), calls=%async_computation.5 | async-start | bytes 4730880 | tf_op jit(solution)/shard_map/all_gather | solution.py:194
  436.8 139.2 %all-gather.14.cloned.1.call-start = ((), (), s32[]{:S(2)}) async-start(), calls=%async_computation.6 | async-start | bytes 4730880 | tf_op jit(solution)/shard_map/all_gather | solution.py:200
  437.4 183.4 %reduce-scatter.2.cloned.1.call-start = ((), (), s32[]{:S(2)}) async-start(), calls=%async_computation.7 | async-start | bytes 3276800 | tf_op jit(solution)/shard_map/reduce_scatter | solution.py:203
  576.0 47.1 %copy-start.1 = (bf16[768,1920]{1,0:T(8,128)(2,1)S(1)}, bf16[768,1920]{1,0:T(8,128)(2,1)}, u32[]{:S(2)}) copy-start(bf16[768,1920]{1,0:T(8,128)(2,1)} %param.29) | copy-start | bytes 8847364
Sparse Core Ops, SparseCore 0:
  10.3 52.7 all-gather.5
  85.0 139.8 all-gather.9
  436.4 42.0 all-gather.7
  480.7 47.2 all-gather.11
  530.2 45.8 all-gather.13
  588.0 32.7 reduce-scatter.1
